TPU v7x, 256 devices: a whole 4x4x8 slice. The times are simulated.
256 devices in a mesh: dp: 32 (over y, z), mp: 8 (over x, core).
Axes of the slice: x: 4, y: 4, z: 8, core: 2. Of those that a mesh axis runs over, the one named last changes fastest.
Arguments:
- hidden: bfloat16 [512, 32, 1024], P(('dp', 'mp')), may hold values from -96 to 96, as said below
- query_weight: bfloat16 [1024, 1024], P('dp', 'mp'), may hold values from -0.1875 to 0.1875
- w_key: bfloat16 [1024, 1024], P('dp', 'mp'), may hold values from -0.1875 to 0.1875
- w_value: bfloat16 [1024, 1024], P('dp', 'mp'), may hold values from -0.1875 to 0.1875
- rel_table: bfloat16 [512, 1024], P('dp'), may hold values from -6 to 6
- rel_bucket: int32 [32, 32], replicated, may hold values from 0 to 511
- w_out: bfloat16 [1024, 1024], P('mp', 'dp'), may hold values from -0.1875 to 0.1875
- w_up: bfloat16 [1024, 4096], P('dp', 'mp'), may hold values from -0.1875 to 0.1875
- w_down: bfloat16 [4096, 1024], P('mp', 'dp'), may hold values from -0.09375 to 0.09375
- w_proj: bfloat16 [1024, 128], P(('dp', 'mp')), may hold values from -0.1875 to 0.1875
- pages: bfloat16 [8192, 128, 128], P('dp'), may hold values from -0.59765625 to 0.59765625
- page_len: int32 [8192], P('dp'), may hold values from 1 to 128
- slot_per_page: int32 [8192], replicated, may hold values from 0 to 8191, as said below
- candidates: int32 [512, 16, 4], P(('dp', 'mp')), may hold values from 0 to 8191, as said below
Outputs:
- query_vectors: bfloat16 [512, 32, 128], P(('dp', 'mp'))
- scores: float32 [512, 16], P(('dp', 'mp'))
Inputs may be any that keep to these rules, and one draw needn't show every extreme that they name: slot_per_page is a permutation of the slots; the page in slot s is held by index s // 256 of dp. `candidates`: among the 128 page ids of the 2 queries of one device (queries in aligned blocks of 2), at most 8 have slots held by any one index of dp, and in every such block some index of dp holds exactly 8 of them. `hidden`: token states are finite.
All inputs are finite; a program needn't handle non-finite values.
Results may differ from a plain program's by a relative error of at most 0.025.
Values may be sent and summed in bfloat16 or wider, within the bound.
No kernel may reach another device: no remote copies, remote signals or barrier semaphores. Data moves between devices by JAX's collectives and lax.ppermute only.
A program may use at most 64 MiB of HBM per device.

v0:
```python
import jax
import jax.numpy as jnp
from jax import lax
from jax.sharding import PartitionSpec as P

HD = 64


def layer_norm(value):
    mean = jnp.mean(value, axis=-1, keepdims=True)
    centered = value - mean
    var = jnp.mean(centered * centered, axis=-1, keepdims=True)
    return centered / jnp.sqrt(var + 1e-07)


def add_rows(left, piece):
    return jnp.dot(left, piece, preferred_element_type=jnp.float32)


def return_maxima(maxima):
    return lax.all_to_all(
        maxima.astype(jnp.bfloat16), "dp", split_axis=0, concat_axis=0, tiled=True
    ).astype(maxima.dtype)


def body(
    hidden,
    query_weight,
    w_key,
    w_value,
    rel_table,
    rel_bucket,
    w_out,
    w_up,
    w_down,
    w_proj,
    pages,
    page_len,
    slot_per_page,
    candidates,
):
    qry_dev, qlen, width = hidden.shape
    heads_local = query_weight.shape[1] // HD
    cols = query_weight.shape[1]
    page_owners = lax.axis_size("dp")
    n_mp = lax.axis_size("mp")
    pg_dev = pages.shape[0]
    ptok = pages.shape[1]
    ncand, ppc = (candidates.shape[1], candidates.shape[2])
    req = qry_dev * ncand * ppc
    cap = 2 * req // page_owners
    slots = slot_per_page[candidates.reshape(req)]
    dest = slots // pg_dev
    local = slots % pg_dev
    query_of = jnp.arange(req, dtype=jnp.int32) // (ncand * ppc)
    member = (dest[:, None] == jnp.arange(page_owners, dtype=jnp.int32)[None, :]).astype(jnp.int32)
    place = jnp.sum((jnp.cumsum(member, axis=0) - 1) * member, axis=1)
    index = dest * cap + place
    codes = jnp.full((page_owners * cap,), -1, jnp.int32).at[index].set(query_of * pg_dev + local)
    codes = codes.reshape(page_owners, cap)
    got = lax.all_to_all(codes, "dp", split_axis=0, concat_axis=0, tiled=True)
    where_local = got % pg_dev
    which_query = jnp.clip(got // pg_dev, 0, qry_dev - 1)
    chosen = pages[where_local]
    lens = page_len[where_local]
    w_out_t = w_out.T
    w_down_t = w_down.T
    pieces = (query_weight, w_key, w_value, w_out_t, w_up, w_down_t, rel_table, w_proj)
    flat_pieces = jnp.concatenate([p.reshape(-1) for p in pieces])
    gathered = lax.all_gather(flat_pieces, "dp", axis=0, tiled=False)
    parts = []
    start = 0
    for p in pieces:
        size = p.size
        parts.append(gathered[:, start : start + size].reshape((page_owners,) + p.shape))
        start += size
    g_q, g_k, g_v, g_out, g_up, g_down, g_rel, g_proj = parts
    wq = g_q.reshape(page_owners * query_weight.shape[0], cols)
    wk = g_k.reshape(page_owners * w_key.shape[0], cols)
    wv = g_v.reshape(page_owners * w_value.shape[0], cols)
    wo = jnp.transpose(g_out, (2, 0, 1)).reshape(w_out.shape[0], page_owners * w_out.shape[1])
    wu = g_up.reshape(page_owners * w_up.shape[0], w_up.shape[1])
    wd = jnp.transpose(g_down, (2, 0, 1)).reshape(w_down.shape[0], page_owners * w_down.shape[1])
    left_rel = g_rel.reshape(page_owners * rel_table.shape[0], rel_table.shape[1])
    proj_all = lax.all_gather(g_proj, "mp", axis=0, tiled=False)
    wp = jnp.transpose(proj_all, (1, 0, 2, 3)).reshape(
        page_owners * n_mp * w_proj.shape[0], w_proj.shape[1]
    )
    tokens = lax.all_gather(hidden, "mp", axis=0, tiled=True)
    group = tokens.shape[0]
    flat = tokens.reshape(group * qlen, width)
    qsum = add_rows(flat, wq)
    ksum = add_rows(flat, wk)
    vsum = add_rows(flat, wv)
    qrsum = add_rows(left_rel, wq)
    krsum = add_rows(left_rel, wk)
    rel_q = qrsum.astype(jnp.bfloat16)
    rel_k = krsum.astype(jnp.bfloat16)
    nbuck = rel_q.shape[0]
    qx = qsum.astype(jnp.bfloat16).reshape(group, qlen, heads_local, HD)
    kx = ksum.astype(jnp.bfloat16).reshape(group, qlen, heads_local, HD)
    vx = vsum.astype(jnp.bfloat16).reshape(group, qlen, heads_local, HD)
    rel_q = rel_q.reshape(nbuck, heads_local, HD)
    rel_k = rel_k.reshape(nbuck, heads_local, HD)
    onehot = (rel_bucket[:, :, None] == jnp.arange(nbuck, dtype=jnp.int32)[None, None, :]).astype(
        jnp.float32
    )
    scale = 1.0 / jnp.sqrt(jnp.float32(3 * HD))
    content = jnp.einsum("qihd,qjhd->qhij", qx, kx, preferred_element_type=jnp.float32)
    along_axis_name = jnp.einsum("qihd,bhd->qhib", qx, rel_k, preferred_element_type=jnp.float32)
    c2p = jnp.einsum("qhib,ijb->qhij", along_axis_name, onehot, precision=lax.Precision.HIGHEST)
    back = jnp.einsum("qjhd,bhd->qhjb", kx, rel_q, preferred_element_type=jnp.float32)
    p2c = jnp.einsum("qhjb,jib->qhij", back, onehot, precision=lax.Precision.HIGHEST)
    logits = (content + c2p + p2c) * scale
    probs = jax.nn.softmax(logits, axis=-1).astype(jnp.bfloat16)
    context_rows = jnp.einsum("qhij,qjhd->qihd", probs, vx, preferred_element_type=jnp.float32)
    context_rows = context_rows.astype(jnp.bfloat16).reshape(group * qlen, cols)
    attn_terms = jnp.dot(context_rows, wo, preferred_element_type=jnp.float32)
    attn = lax.psum_scatter(
        attn_terms.astype(jnp.bfloat16), "mp", scatter_dimension=0, tiled=True
    ).astype(jnp.float32)
    own = hidden.reshape(qry_dev * qlen, width).astype(jnp.float32)
    mid = layer_norm(own + attn).astype(jnp.bfloat16)
    mid_all = lax.all_gather(mid, "mp", axis=0, tiled=True)
    up = add_rows(mid_all, wu)
    inner = jax.nn.gelu(up, approximate=False).astype(jnp.bfloat16)
    down_terms = jnp.dot(inner, wd, preferred_element_type=jnp.float32)
    mlp = lax.psum_scatter(
        down_terms.astype(jnp.bfloat16), "mp", scatter_dimension=0, tiled=True
    ).astype(jnp.float32)
    state = layer_norm(mid.astype(jnp.float32) + mlp).astype(jnp.bfloat16)
    width_out = w_proj.shape[1]
    proj = add_rows(state, wp)
    vectors = (proj / jnp.sqrt(jnp.sum(proj * proj, axis=-1, keepdims=True) + 1e-06)).astype(
        jnp.bfloat16
    )
    vectors = vectors.reshape(qry_dev, qlen, width_out)
    sent = jnp.broadcast_to(vectors[None], (page_owners, qry_dev, qlen, width_out))
    recv = lax.all_to_all(sent, "dp", split_axis=0, concat_axis=0, tiled=True)
    rows_in = jnp.take_along_axis(recv, which_query[:, :, None, None], axis=1)
    token_positions = jnp.arange(ptok, dtype=jnp.int32)
    sim = jnp.einsum("snie,snte->snit", rows_in, chosen, preferred_element_type=jnp.float32)
    valid = token_positions[None, None, None, :] < lens[:, :, None, None]
    returned = return_maxima(jnp.max(jnp.where(valid, sim, -1e30), axis=-1))
    best = returned.reshape(page_owners * cap, qlen)[index]
    best = best.reshape(qry_dev, ncand, ppc, qlen)
    scores = jnp.sum(jnp.max(best, axis=2), axis=-1)
    return (vectors, scores)


def solution(mesh):
    in_specs = (
        P(("dp", "mp"), None, None),
        P("dp", "mp"),
        P("dp", "mp"),
        P("dp", "mp"),
        P("dp", None),
        P(),
        P("mp", "dp"),
        P("dp", "mp"),
        P("mp", "dp"),
        P(("dp", "mp"), None),
        P("dp", None, None),
        P("dp"),
        P(),
        P(("dp", "mp"), None, None),
    )
    out_specs = (P(("dp", "mp"), None, None), P(("dp", "mp"), None))
    return jax.shard_map(body, mesh=mesh, in_specs=in_specs, out_specs=out_specs, check_vma=False)
```

profile of v0, /device:TPU:8, one launch (start us, length us, event | category | flops | bytes accessed | tf_op | source)
XLA Modules:
  0.0 330.8 jit_solution(3690136183016734294)
XLA Ops:
  7.2 0.7 bitcast_dynamic-update-slice_fusion.3
  7.9 0.8 copy.68
  8.7 0.8 copy.69
  9.5 0.8 copy.70
  10.2 0.7 bitcast_dynamic-update-slice_fusion.2
  10.9 0.7 bitcast_dynamic-update-slice_fusion.1
  11.6 0.7 bitcast_dynamic-update-slice_fusion
  12.4 0.7 constant_dynamic-update-slice_fusion
  13.0 0.8 reshape.444
  13.9 0.7 all-gather.6.cloned.1.call-update
  14.7 99.2 %all-gather.10.cloned.1.call-done = bf16[32,1,66048]{2,1,0:T(2,128)(2,1)} async-done(((bf16[1,1,66048]{2,1,0:T(2,128)(2,1)}), bf16[32,1,66048]{2,1,0:T(2,128)(2,1)}) %all-gather.10.cloned.1.call-update) | async-done | bytes 4227088 | tf_op jit(solution)/shard_map/all_gather | solution.py:70
  113.9 3.9 %copy.85 = bf16[32,1,66048]{2,0,1:T(8,128)(2,1)S(1)} copy(bf16[32,1,66048]{2,1,0:T(2,128)(2,1)} %all-gather.10.cloned.1.call-done) | data formatting | bytes 8454144
  117.8 1.5 fusion.123
  119.3 0.8 copy-done.2
  120.1 0.9 slice_bitcast_fusion
  121.1 1.6 reshape_reshape.18
  122.7 1.8 reshape_reshape.17
  124.5 1.1 convolution_convert_fusion.3
  125.6 2.1 convolution_convert_fusion.4
  127.7 12.2 %all-gather.6.cloned.1.call-done = bf16[16,32,1024]{2,1,0:T(8,128)(2,1)} async-done(((bf16[2,32,1024]{2,1,0:T(8,128)(2,1)}), bf16[16,32,1024]{2,1,0:T(8,128)(2,1)}) %all-gather.6.cloned.1.call-update) | async-done | bytes 1048592 | tf_op jit(solution)/shard_map/all_gather | solution.py:89
  139.9 1.8 fusion.17
  141.8 1.7 fusion.16
  144.1 0.5 fusion.63
  144.6 2.2 fusion.1
  146.7 0.5 fusion.65
  147.2 2.2 fusion.3
  149.4 2.2 copy.56
  151.7 1.7 fusion.13
  153.6 0.6 copy-done.8
  154.2 1.1 reshape_reshape.15
  155.3 1.1 fusion.15
  156.4 1.1 copy.50
  157.6 1.5 fusion.14
  159.2 0.2 copy.61
  159.6 1.4 convolution_convert_fusion
  161.1 34.7 %reduce-scatter.3.cloned.1.call-done = bf16[64,1024]{1,0:T(8,128)(2,1)} async-done(((bf16[512,1024]{1,0:T(8,128)(2,1)}), bf16[64,1024]{1,0:T(8,128)(2,1)}) %reduce-scatter.3.cloned.1.call-update) | async-done | bytes 131088 | tf_op jit(solution)/shard_map/reduce_scatter | solution.py:119
  195.9 1.0 fusion.73
  196.9 1.1 multiply_reduce_fusion.1
  198.0 1.7 divide_convert_fusion.3
  200.0 0.3 copy.72
  200.3 0.5 reshape_reshape.19
  200.8 23.7 %all-gather.8.cloned.1.call-done = bf16[512,1024]{1,0:T(8,128)(2,1)} async-done(((bf16[64,1024]{1,0:T(8,128)(2,1)}), bf16[512,1024]{1,0:T(8,128)(2,1)}) %all-gather.8.cloned.1.call-update) | async-done | bytes 1048592 | tf_op jit(solution)/shard_map/all_gather | solution.py:124
  224.5 5.6 %convolution_convert_fusion.1 = bf16[512,1024]{1,0:T(8,128)(2,1)} fusion(bf16[512,1024]{0,1:T(8,128)(2,1)S(1)} %bitcast.137, bf16[512,1024]{1,0:T(8,128)(2,1)} %all-gather.8.cloned.1.call-done, bf16[1024,512]{1,0:T(8,128)(2,1)S(1)} %reshape_reshape.19), kind=kOutput, calls=%fused_computation.19 | convolution fusion | flops 1091305472 | bytes 4194304 | tf_op jit(solution)/shard_map/dot_general | solution.py:127
  230.4 1.1 gather_fusion
  232.0 1.0 scatter_custom_fusion
  233.0 0.7 all_to_all.16
  233.7 10.1 %all-to-all-start = ((s32[32,1,8]{2,1,0:T(1,128)}), s32[32,1,8]{2,1,0:T(1,128)S(1)}, u32[]{:S(2)}, u32[]{:S(2)}) async-start(s32[32,1,8]{2,1,0:T(1,128)} %bitcast.36), calls=%async_computation.2 | async-start | bytes 32768 | tf_op jit(solution)/shard_map/all_to_all | solution.py:61
  243.8 0.8 slice.49
  244.6 9.9 %all_gather.19 = bf16[8,32,4,128]{3,2,0,1:T(4,128)(2,1)S(1)} all-gather(bf16[1,32,4,128]{3,2,0,1:T(4,128)(2,1)S(1)} %bitcast.145), channel_id=1, replica_groups=mesh['dp'=32,'mp'=8] {'mp'}, dimensions={0}, use_global_device_ids=true | all-gather | bytes 294912 | tf_op jit(solution)/shard_map/all_gather | solution.py:85
  254.5 11.1 %reduce-scatter.5.cloned.1.call-done = bf16[64,1024]{1,0:T(8,128)(2,1)} async-done(((bf16[512,1024]{1,0:T(8,128)(2,1)}), bf16[64,1024]{1,0:T(8,128)(2,1)}) %reduce-scatter.5.cloned.1.call-update) | async-done | bytes 131088 | tf_op jit(solution)/shard_map/reduce_scatter | solution.py:128
  265.6 1.0 fusion.71
  266.6 1.1 multiply_reduce_fusion
  267.7 1.3 multiply_reduce_fusion.2
  269.1 1.0 broadcast_in_dim.21
  270.1 10.0 %all-to-all-start.1 = ((bf16[32,2,32,128]{3,2,1,0:T(8,128)(2,1)}), bf16[32,2,32,128]{3,2,1,0:T(8,128)(2,1)S(1)}, u32[]{:S(2)}, u32[]{:S(2)}) async-start(bf16[32,2,32,128]{3,2,1,0:T(8,128)(2,1)} %broadcast_in_dim.21), calls=%async_computation.3 | async-start | bytes 1048576 | tf_op jit(solution)/shard_map/all_to_all | solution.py:139
  280.3 11.8 %gather_fusion.2 = bf16[256,128,128]{2,1,0:T(8,128)(2,1)} fusion(bf16[256,128,128]{2,1,0:T(8,128)(2,1)} %param.24, s32[1024]{0:T(1024)S(1)} %pad_clamp_fusion.1), kind=kCustom, calls=%fused_computation.2 | custom fusion | bytes 16778240 | tf_op jit(solution)/shard_map/gather | solution.py:64
  292.2 1.9 gather_fusion.1
  294.3 1.3 gather_fusion.4
  295.7 8.0 %select_reduce_fusion = bf16[32,8,32]{2,1,0:T(8,128)(2,1)S(1)} fusion(bf16[32,8,128,128]{3,2,1,0:T(8,128)(2,1)} %bitcast.134, bf16[32,8,32,128]{3,2,1,0:T(8,128)(2,1)S(1)} %bitcast.136, pred[32,8]{1,0:T(8,128)(4,1)S(1)} %compare_and_fusion, pred[32,8,128]{2,1,0:T(8,128)(4,1)S(1)} %iota_compare_fusion.1), kind=kOutput, calls=%fused_computation.8 | convolution fusion | flops 271572992 | bytes 10535168 | tf_op jit(solution)/shard_map/snie,snte->snit/dot_general | solution.py:142
  303.7 0.7 reshape.452
  304.4 9.8 %all-to-all-start.2 = ((bf16[32,2,128]{2,1,0:T(2,128)(2,1)}), bf16[32,2,128]{2,1,0:T(2,128)(2,1)S(1)}, u32[]{:S(2)}, u32[]{:S(2)}) async-start(bf16[32,2,128]{2,1,0:T(2,128)(2,1)} %reshape.452), calls=%async_computation.4 | async-start | bytes 32768 | tf_op jit(solution)/shard_map/all_to_all | solution.py:21
  314.2 8.6 %all-to-all-done.2 = bf16[32,2,128]{2,1,0:T(2,128)(2,1)S(1)} async-done(((bf16[32,2,128]{2,1,0:T(2,128)(2,1)}), bf16[32,2,128]{2,1,0:T(2,128)(2,1)S(1)}, u32[]{:S(2)}, u32[]{:S(2)}) %all-to-all-start.2) | async-done | bytes 16416 | tf_op jit(solution)/shard_map/all_to_all | solution.py:21
  322.9 0.6 gather_fusion.3
  323.6 0.7 reduce_sum.82
  (76 shorter events, 3.0 us)
Async XLA Ops:
  7.2 223.2 %copy-start = (s32[8192]{0:T(1024)S(1)}, s32[8192]{0:T(1024)}, u32[]{:S(2)}) copy-start(s32[8192]{0:T(1024)} %param.26) | copy-start | bytes 98308
  7.2 106.8 %all-gather.10.cloned.1.call-start = ((), (), s32[]{:S(2)}) async-start(), calls=%async_computation.9 | async-start | bytes 8718336 | tf_op jit(solution)/shard_map/all_gather | solution.py:70
  13.9 126.0 %all-gather.6.cloned.1.call-start = ((), (), s32[]{:S(2)}) async-start(), calls=%async_computation.5 | async-start | bytes 1179648 | tf_op jit(solution)/shard_map/all_gather | solution.py:89
  14.7 181.2 %reduce-scatter.3.cloned.1.call-start = ((), (), s32[]{:S(2)}) async-start(), calls=%async_computation.6 | async-start | bytes 1179648 | tf_op jit(solution)/shard_map/reduce_scatter | solution.py:119
  117.8 2.3 copy-start.2
  139.9 4.1 %copy-start.10 = (bf16[512,128]{0,1:T(8,128)(2,1)S(1)}, bf16[512,128]{0,1:T(8,128)(2,1)}, u32[]{:S(2)}) copy-start(bf16[512,128]{0,1:T(8,128)(2,1)} %convolution_convert_fusion.3) | copy-start | bytes 393220
  143.5 1.1 copy-start.11
  144.0 2.7 copy-start.4
  144.1 2.7 copy-start.9
  149.4 5.8 %copy-start.3 = (bf16[16,32,1024]{2,1,0:T(8,128)(2,1)S(1)}, bf16[16,32,1024]{2,1,0:T(8,128)(2,1)}, u32[]{:S(2)}) copy-start(bf16[16,32,1024]{2,1,0:T(8,128)(2,1)} %all-gather.6.cloned.1.call-done) | copy-start | bytes 3145732
  153.4 0.8 copy-start.8
  156.4 3.2 copy-start.7
  159.2 36.7 %copy-start.5 = (bf16[2,32,1024]{2,1,0:T(8,128)(2,1)S(1)}, bf16[2,32,1024]{2,1,0:T(8,128)(2,1)}, u32[]{:S(2)}) copy-start(bf16[2,32,1024]{2,1,0:T(8,128)(2,1)} %param.14) | copy-start | bytes 393220
  161.1 63.5 %all-gather.8.cloned.1.call-start = ((), (), s32[]{:S(2)}) async-start(), calls=%async_computation.7 | async-start | bytes 1179648 | tf_op jit(solution)/shard_map/all_gather | solution.py:124
  199.7 65.8 %reduce-scatter.5.cloned.1.call-start = ((), (), s32[]{:S(2)}) async-start(), calls=%async_computation.8 | async-start | bytes 1179648 | tf_op jit(solution)/shard_map/reduce_scatter | solution.py:128
  224.5 5.6 %copy-start.13 = (s32[2,16,4]{1,2,0:T(4,128)S(1)}, s32[2,16,4]{1,2,0:T(4,128)}, u32[]{:S(2)}) copy-start(s32[2,16,4]{1,2,0:T(4,128)} %param.27) | copy-start | bytes 1540
  230.1 35.4 %copy-start.6 = (bf16[64,1024]{1,0:T(8,128)(2,1)S(1)}, bf16[64,1024]{1,0:T(8,128)(2,1)}, u32[]{:S(2)}) copy-start(bf16[64,1024]{1,0:T(8,128)(2,1)} %divide_convert_fusion.3) | copy-start | bytes 393220
  233.7 35.4 %all-to-all-start = ((s32[32,1,8]{2,1,0:T(1,128)}), s32[32,1,8]{2,1,0:T(1,128)S(1)}, u32[]{:S(2)}, u32[]{:S(2)}) async-start(s32[32,1,8]{2,1,0:T(1,128)} %bitcast.36), calls=%async_computation.2 | async-start | bytes 32768 | tf_op jit(solution)/shard_map/all_to_all | solution.py:61
  269.1 23.1 %copy-start.12 = (bf16[64,128]{1,0:T(8,128)(2,1)}, bf16[64,128]{1,0:T(8,128)(2,1)S(1)}, u32[]{:S(2)}) copy-start(bf16[64,128]{1,0:T(8,128)(2,1)S(1)} %divide_convert_fusion.5) | copy-start | bytes 49156
  270.1 24.2 %all-to-all-start.1 = ((bf16[32,2,32,128]{3,2,1,0:T(8,128)(2,1)}), bf16[32,2,32,128]{3,2,1,0:T(8,128)(2,1)S(1)}, u32[]{:S(2)}, u32[]{:S(2)}) async-start(bf16[32,2,32,128]{3,2,1,0:T(8,128)(2,1)} %broadcast_in_dim.21), calls=%async_computation.3 | async-start | bytes 1048576 | tf_op jit(solution)/shard_map/all_to_all | solution.py:139
  280.3 11.9 %copy-start.1 = (s32[256]{0:T(256)S(1)}, s32[256]{0:T(256)}, u32[]{:S(2)}) copy-start(s32[256]{0:T(256)} %param.25) | copy-start | bytes 3076
  304.4 18.4 %all-to-all-start.2 = ((bf16[32,2,128]{2,1,0:T(2,128)(2,1)}), bf16[32,2,128]{2,1,0:T(2,128)(2,1)S(1)}, u32[]{:S(2)}, u32[]{:S(2)}) async-start(bf16[32,2,128]{2,1,0:T(2,128)(2,1)} %reshape.452), calls=%async_computation.4 | async-start | bytes 32768 | tf_op jit(solution)/shard_map/all_to_all | solution.py:21
Sparse Core Ops, SparseCore 0:
  14.0 99.8 all-gather.9
  115.8 24.0 all-gather.5
  161.2 34.6 reduce-scatter.2
  199.9 24.6 all-gather.7
  230.3 35.2 reduce-scatter.4
where the time goes:
time: 332 us; the launch traced here: 331 us
  waiting for transfers between devices  190 us (57%)
  local copies, waits for them, and re-layouts  45.7 us (14%)
  matrix products  32.7 us (10%)
  starting transfers between devices  30.3 us (9%)
  between operations  14.3 us (4%)
  blocking collectives  9.85 us (3%)
  other arithmetic  7.6 us (2%)
    all_gather x1, waiting for transfers between devices, body(): gathered = lax.all_gather(flat_pieces, 'dp', axis=0, tiled=False)  99.2 us
    reduce_scatter x1, waiting for transfers between devices, body(): lax.psum_scatter(attn_terms.astype(jnp.bfloat16), 'mp', scatter_dimension...  34.7 us
    all_gather x1, waiting for transfers between devices, body(): mid_all = lax.all_gather(mid, 'mp', axis=0, tiled=True)  23.7 us
    unnamed x46, local copies, waits for them, and re-layouts  13.4 us
    all_gather x1, waiting for transfers between devices, body(): tokens = lax.all_gather(hidden, 'mp', axis=0, tiled=True)  12.2 us
    gather x1, local copies, waits for them, and re-layouts, body(): chosen = pages[where_local]  11.8 us
    reduce_scatter x1, waiting for transfers between devices, body(): lax.psum_scatter(down_terms.astype(jnp.bfloat16), 'mp', scatter_dimension...  11.1 us
    all_to_all x1, starting transfers between devices, body(): got = lax.all_to_all(codes, 'dp', split_axis=0, concat_axis=0, tiled=True)  10.1 us
  transfers between devices with their start and end apart: 8, of which 6 were waited for; matrix products, arithmetic and copies ran while one was open for 11% of the time, Pallas kernels for 0%

commit v1 on v0

--- a/solution.py
+++ b/solution.py
@@ -86,7 +86,10 @@
     wp = jnp.transpose(proj_all, (1, 0, 2, 3)).reshape(
         page_owners * n_mp * w_proj.shape[0], w_proj.shape[1]
     )
-    tokens = lax.all_gather(hidden, "mp", axis=0, tiled=True)
+    tokens_switch = lambda sample, where_dim: jnp.concatenate(
+        lax.all_to_all(jnp.stack([sample] * lax.axis_size("mp")), "mp", 0, 0), axis=where_dim
+    )
+    tokens = tokens_switch(hidden, 0)
     group = tokens.shape[0]
     flat = tokens.reshape(group * qlen, width)
     qsum = add_rows(flat, wq)

time: 332 us -> 312 us (0.940)
  waiting for transfers between devices: 190 us -> 170 us
  starting transfers between devices: 30.3 us -> 34.5 us
    all_gather x1 -> x0, waiting for transfers between devices: 12.2 us -> none  [body(): tokens = lax.all_gather(hidden, 'mp', axis=0, tiled=True)]
    all_gather x1, waiting for transfers between devices: 99.2 us -> 93.6 us  [body(): gathered = lax.all_gather(flat_pieces, 'dp', axis=0, tiled=False)]
    all_to_all x0 -> x1, starting transfers between devices: none -> 4.3 us  [body(): lax.all_to_all(jnp.stack([sample] * lax.axis_size('mp')), 'mp', 0, 0)]
  transfers between devices with their start and end apart: 8 -> 8, of which waited for: 6 -> 5; matrix products, arithmetic and copies ran while one was open for 11% -> 12% of each run, Pallas kernels for 0% -> 0%
where the time goes in v1:
time: 312 us; the launch traced here: 311 us
  waiting for transfers between devices  170 us (54%)
  local copies, waits for them, and re-layouts  44.9 us (14%)
  starting transfers between devices  34.5 us (11%)
  matrix products  29.7 us (10%)
  between operations  14.3 us (5%)
  blocking collectives  9.85 us (3%)
  other arithmetic  7.6 us (2%)
    all_gather x1, waiting for transfers between devices, body(): gathered = lax.all_gather(flat_pieces, 'dp', axis=0, tiled=False)  93.6 us
    reduce_scatter x1, waiting for transfers between devices, body(): lax.psum_scatter(attn_terms.astype(jnp.bfloat16), 'mp', scatter_dimension...  33.1 us
    all_gather x1, waiting for transfers between devices, body(): mid_all = lax.all_gather(mid, 'mp', axis=0, tiled=True)  23.7 us
    unnamed x46, local copies, waits for them, and re-layouts  13.3 us
    gather x1, local copies, waits for them, and re-layouts, body(): chosen = pages[where_local]  11.8 us
    reduce_scatter x1, waiting for transfers between devices, body(): lax.psum_scatter(down_terms.astype(jnp.bfloat16), 'mp', scatter_dimension...  11.1 us
    all_to_all x1, starting transfers between devices, body(): got = lax.all_to_all(codes, 'dp', split_axis=0, concat_axis=0, tiled=True)  10.1 us
    all_to_all x1, starting transfers between devices, body(): recv = lax.all_to_all(sent, 'dp', split_axis=0, concat_axis=0, tiled=True)  9.96 us
  transfers between devices with their start and end apart: 8, of which 5 were waited for; matrix products, arithmetic and copies ran while one was open for 12% of the time, Pallas kernels for 0%

profile of v1, /device:TPU:8, one launch (start us, length us, event | category | flops | bytes accessed | tf_op | source)
XLA Modules:
  0.0 311.2 jit_solution(2329518231415601937)
XLA Ops:
  7.2 0.7 bitcast_dynamic-update-slice_fusion.3
  7.9 0.8 copy.68
  8.7 0.8 copy.69
  9.5 0.8 copy.70
  10.2 0.7 bitcast_dynamic-update-slice_fusion.2
  10.9 0.7 bitcast_dynamic-update-slice_fusion.1
  11.6 0.7 bitcast_dynamic-update-slice_fusion
  12.4 0.7 constant_dynamic-update-slice_fusion
  13.0 0.8 reshape.442
  13.9 2.1 stack.2
  16.0 4.3 %all-to-all-start = ((bf16[8,2,32,1024]{3,2,1,0:T(8,128)(2,1)}), bf16[8,2,32,1024]{3,2,1,0:T(8,128)(2,1)S(1)}, u32[]{:S(2)}, u32[]{:S(2)}) async-start(bf16[8,2,32,1024]{3,2,1,0:T(8,128)(2,1)} %stack.2), calls=%async_computation | async-start | bytes 2097152 | tf_op jit(solution)/shard_map/all_to_all | solution.py:90
  20.3 93.6 %all-gather.7.cloned.1.call-done = bf16[32,1,66048]{2,1,0:T(2,128)(2,1)} async-done(((bf16[1,1,66048]{2,1,0:T(2,128)(2,1)}), bf16[32,1,66048]{2,1,0:T(2,128)(2,1)}) %all-gather.7.cloned.1.call-update) | async-done | bytes 4227088 | tf_op jit(solution)/shard_map/all_gather | solution.py:70
  113.9 3.9 %copy.85 = bf16[32,1,66048]{2,0,1:T(8,128)(2,1)S(1)} copy(bf16[32,1,66048]{2,1,0:T(2,128)(2,1)} %all-gather.7.cloned.1.call-done) | data formatting | bytes 8454144
  117.8 1.9 fusion.123
  119.7 0.8 copy-done.2
  120.4 0.9 slice_bitcast_fusion
  121.5 1.6 reshape_reshape.22
  123.0 1.8 reshape_reshape.21
  124.8 1.2 convolution_convert_fusion.3
  126.0 2.1 convolution_convert_fusion.4
  128.0 1.5 fusion.17
  129.5 0.5 fusion.16
  130.6 0.5 fusion.63
  131.1 2.2 fusion.1
  133.3 0.5 fusion.65
  133.8 1.4 fusion.3
  135.2 1.1 copy.56
  136.3 1.6 fusion.13
  137.9 0.2 fusion.124
  138.3 0.5 copy-done.8
  138.7 0.5 fusion.15
  139.5 1.5 fusion.14
  141.1 0.2 copy.61
  141.5 1.4 convolution_convert_fusion
  143.1 33.1 %reduce-scatter.3.cloned.1.call-done = bf16[64,1024]{1,0:T(8,128)(2,1)} async-done(((bf16[512,1024]{1,0:T(8,128)(2,1)}), bf16[64,1024]{1,0:T(8,128)(2,1)}) %reduce-scatter.3.cloned.1.call-update) | async-done | bytes 131088 | tf_op jit(solution)/shard_map/reduce_scatter | solution.py:122
  176.2 1.0 fusion.73
  177.3 1.1 multiply_reduce_fusion.1
  178.4 1.7 divide_convert_fusion.3
  180.1 0.2 reduce-scatter.5.cloned.1.call-start
  180.3 0.3 copy.72
  180.7 0.5 reshape_reshape.23
  181.2 23.7 %all-gather.5.cloned.1.call-done = bf16[512,1024]{1,0:T(8,128)(2,1)} async-done(((bf16[64,1024]{1,0:T(8,128)(2,1)}), bf16[512,1024]{1,0:T(8,128)(2,1)}) %all-gather.5.cloned.1.call-update) | async-done | bytes 1048592 | tf_op jit(solution)/shard_map/all_gather | solution.py:127
  204.9 5.6 %convolution_convert_fusion.1 = bf16[512,1024]{1,0:T(8,128)(2,1)} fusion(bf16[512,1024]{0,1:T(8,128)(2,1)S(1)} %bitcast.137, bf16[512,1024]{1,0:T(8,128)(2,1)} %all-gather.5.cloned.1.call-done, bf16[1024,512]{1,0:T(8,128)(2,1)S(1)} %reshape_reshape.23), kind=kOutput, calls=%fused_computation.19 | convolution fusion | flops 1091305472 | bytes 4194304 | tf_op jit(solution)/shard_map/dot_general | solution.py:130
  210.8 1.1 gather_fusion
  212.4 1.0 scatter_custom_fusion
  213.4 0.7 all_to_all.20
  214.1 10.1 %all-to-all-start.1 = ((s32[32,1,8]{2,1,0:T(1,128)}), s32[32,1,8]{2,1,0:T(1,128)S(1)}, u32[]{:S(2)}, u32[]{:S(2)}) async-start(s32[32,1,8]{2,1,0:T(1,128)} %bitcast.36), calls=%async_computation.3 | async-start | bytes 32768 | tf_op jit(solution)/shard_map/all_to_all | solution.py:61
  224.2 0.8 slice.49
  225.0 9.9 %all_gather.15 = bf16[8,32,4,128]{3,2,0,1:T(4,128)(2,1)S(1)} all-gather(bf16[1,32,4,128]{3,2,0,1:T(4,128)(2,1)S(1)} %bitcast.145), channel_id=1, replica_groups=mesh['dp'=32,'mp'=8] {'mp'}, dimensions={0}, use_global_device_ids=true | all-gather | bytes 294912 | tf_op jit(solution)/shard_map/all_gather | solution.py:85
  234.8 11.1 %reduce-scatter.5.cloned.1.call-done = bf16[64,1024]{1,0:T(8,128)(2,1)} async-done(((bf16[512,1024]{1,0:T(8,128)(2,1)}), bf16[64,1024]{1,0:T(8,128)(2,1)}) %reduce-scatter.5.cloned.1.call-update) | async-done | bytes 131088 | tf_op jit(solution)/shard_map/reduce_scatter | solution.py:131
  245.9 1.0 fusion.71
  247.0 1.1 multiply_reduce_fusion
  248.1 1.3 multiply_reduce_fusion.2
  249.5 1.0 broadcast_in_dim.21
  250.5 10.0 %all-to-all-start.2 = ((bf16[32,2,32,128]{3,2,1,0:T(8,128)(2,1)}), bf16[32,2,32,128]{3,2,1,0:T(8,128)(2,1)S(1)}, u32[]{:S(2)}, u32[]{:S(2)}) async-start(bf16[32,2,32,128]{3,2,1,0:T(8,128)(2,1)} %broadcast_in_dim.21), calls=%async_computation.4 | async-start | bytes 1048576 | tf_op jit(solution)/shard_map/all_to_all | solution.py:142
  260.7 11.8 %gather_fusion.2 = bf16[256,128,128]{2,1,0:T(8,128)(2,1)} fusion(bf16[256,128,128]{2,1,0:T(8,128)(2,1)} %param.24, s32[1024]{0:T(1024)S(1)} %pad_clamp_fusion.1), kind=kCustom, calls=%fused_computation.2 | custom fusion | bytes 16778240 | tf_op jit(solution)/shard_map/gather | solution.py:64
  272.5 1.9 gather_fusion.1
  274.7 1.3 gather_fusion.4
  276.0 8.0 %select_reduce_fusion = bf16[32,8,32]{2,1,0:T(8,128)(2,1)S(1)} fusion(bf16[32,8,128,128]{3,2,1,0:T(8,128)(2,1)} %bitcast.134, bf16[32,8,32,128]{3,2,1,0:T(8,128)(2,1)S(1)} %bitcast.136, pred[32,8]{1,0:T(8,128)(4,1)S(1)} %compare_and_fusion, pred[32,8,128]{2,1,0:T(8,128)(4,1)S(1)} %iota_compare_fusion.1), kind=kOutput, calls=%fused_computation.8 | convolution fusion | flops 271572992 | bytes 10535168 | tf_op jit(solution)/shard_map/snie,snte->snit/dot_general | solution.py:145
  284.1 0.7 reshape.450
  284.8 9.8 %all-to-all-start.3 = ((bf16[32,2,128]{2,1,0:T(2,128)(2,1)}), bf16[32,2,128]{2,1,0:T(2,128)(2,1)S(1)}, u32[]{:S(2)}, u32[]{:S(2)}) async-start(bf16[32,2,128]{2,1,0:T(2,128)(2,1)} %reshape.450), calls=%async_computation.5 | async-start | bytes 32768 | tf_op jit(solution)/shard_map/all_to_all | solution.py:21
  294.6 8.6 %all-to-all-done.3 = bf16[32,2,128]{2,1,0:T(2,128)(2,1)S(1)} async-done(((bf16[32,2,128]{2,1,0:T(2,128)(2,1)}), bf16[32,2,128]{2,1,0:T(2,128)(2,1)S(1)}, u32[]{:S(2)}, u32[]{:S(2)}) %all-to-all-start.3) | async-done | bytes 16416 | tf_op jit(solution)/shard_map/all_to_all | solution.py:21
  303.3 0.6 gather_fusion.3
  304.0 0.7 reduce_sum.82
  (76 shorter events, 2.8 us)
Async XLA Ops:
  7.2 203.6 %copy-start = (s32[8192]{0:T(1024)S(1)}, s32[8192]{0:T(1024)}, u32[]{:S(2)}) copy-start(s32[8192]{0:T(1024)} %param.26) | copy-start | bytes 98308
  7.2 106.8 %all-gather.7.cloned.1.call-start = ((), (), s32[]{:S(2)}) async-start(), calls=%async_computation.9 | async-start | bytes 8718336 | tf_op jit(solution)/shard_map/all_gather | solution.py:70
  16.0 112.1 %all-to-all-start = ((bf16[8,2,32,1024]{3,2,1,0:T(8,128)(2,1)}), bf16[8,2,32,1024]{3,2,1,0:T(8,128)(2,1)S(1)}, u32[]{:S(2)}, u32[]{:S(2)}) async-start(bf16[8,2,32,1024]{3,2,1,0:T(8,128)(2,1)} %stack.2), calls=%async_computation | async-start | bytes 2097152 | tf_op jit(solution)/shard_map/all_to_all | solution.py:90
  20.3 155.9 %reduce-scatter.3.cloned.1.call-start = ((), (), s32[]{:S(2)}) async-start(), calls=%async_computation.6 | async-start | bytes 1179648 | tf_op jit(solution)/shard_map/reduce_scatter | solution.py:122
  117.8 2.6 copy-start.2
  128.0 2.5 copy-start.10
  130.0 1.1 copy-start.11
  130.6 2.7 copy-start.9
  135.2 3.0 copy-start.7
  137.9 0.8 copy-start.8
  139.2 2.2 copy-start.6
  141.1 35.2 %copy-start.4 = (bf16[2,32,1024]{2,1,0:T(8,128)(2,1)S(1)}, bf16[2,32,1024]{2,1,0:T(8,128)(2,1)}, u32[]{:S(2)}) copy-start(bf16[2,32,1024]{2,1,0:T(8,128)(2,1)} %param.14) | copy-start | bytes 393220
  141.5 38.8 %copy-start.3 = (bf16[32,16384]{1,0:T(8,128)(2,1)S(1)}, bf16[32,16384]{1,0:T(8,128)(2,1)}, u32[]{:S(2)}) copy-start(bf16[32,16384]{1,0:T(8,128)(2,1)} %get-tuple-element.3) | copy-start | bytes 3145732
  143.0 61.9 %all-gather.5.cloned.1.call-start = ((), (), s32[]{:S(2)}) async-start(), calls=%async_computation.7 | async-start | bytes 1179648 | tf_op jit(solution)/shard_map/all_gather | solution.py:127
  180.1 65.8 %reduce-scatter.5.cloned.1.call-start = ((), (), s32[]{:S(2)}) async-start(), calls=%async_computation.8 | async-start | bytes 1179648 | tf_op jit(solution)/shard_map/reduce_scatter | solution.py:131
  204.9 5.6 %copy-start.13 = (s32[2,16,4]{1,2,0:T(4,128)S(1)}, s32[2,16,4]{1,2,0:T(4,128)}, u32[]{:S(2)}) copy-start(s32[2,16,4]{1,2,0:T(4,128)} %param.27) | copy-start | bytes 1540
  210.5 35.4 %copy-start.5 = (bf16[64,1024]{1,0:T(8,128)(2,1)S(1)}, bf16[64,1024]{1,0:T(8,128)(2,1)}, u32[]{:S(2)}) copy-start(bf16[64,1024]{1,0:T(8,128)(2,1)} %divide_convert_fusion.3) | copy-start | bytes 393220
  214.1 35.4 %all-to-all-start.1 = ((s32[32,1,8]{2,1,0:T(1,128)}), s32[32,1,8]{2,1,0:T(1,128)S(1)}, u32[]{:S(2)}, u32[]{:S(2)}) async-start(s32[32,1,8]{2,1,0:T(1,128)} %bitcast.36), calls=%async_computation.3 | async-start | bytes 32768 | tf_op jit(solution)/shard_map/all_to_all | solution.py:61
  249.5 23.0 %copy-start.12 = (bf16[64,128]{1,0:T(8,128)(2,1)}, bf16[64,128]{1,0:T(8,128)(2,1)S(1)}, u32[]{:S(2)}) copy-start(bf16[64,128]{1,0:T(8,128)(2,1)S(1)} %divide_convert_fusion.5) | copy-start | bytes 49156
  250.5 24.2 %all-to-all-start.2 = ((bf16[32,2,32,128]{3,2,1,0:T(8,128)(2,1)}), bf16[32,2,32,128]{3,2,1,0:T(8,128)(2,1)S(1)}, u32[]{:S(2)}, u32[]{:S(2)}) async-start(bf16[32,2,32,128]{3,2,1,0:T(8,128)(2,1)} %broadcast_in_dim.21), calls=%async_computation.4 | async-start | bytes 1048576 | tf_op jit(solution)/shard_map/all_to_all | solution.py:142
  260.7 11.9 %copy-start.1 = (s32[256]{0:T(256)S(1)}, s32[256]{0:T(256)}, u32[]{:S(2)}) copy-start(s32[256]{0:T(256)} %param.25) | copy-start | bytes 3076
  284.8 18.4 %all-to-all-start.3 = ((bf16[32,2,128]{2,1,0:T(2,128)(2,1)}), bf16[32,2,128]{2,1,0:T(2,128)(2,1)S(1)}, u32[]{:S(2)}, u32[]{:S(2)}) async-start(bf16[32,2,128]{2,1,0:T(2,128)(2,1)} %reshape.450), calls=%async_computation.5 | async-start | bytes 32768 | tf_op jit(solution)/shard_map/all_to_all | solution.py:21
Sparse Core Ops, SparseCore 0:
  14.0 99.8 all-gather.6
  143.1 33.0 reduce-scatter.2
  180.2 24.6 all-gather.4
  210.6 35.2 reduce-scatter.4
